TPU v7x, 128 devices: a whole 4x4x4 slice. The times are simulated.
128 devices in a mesh: ctx: 8 (over x, core), tp: 8 (over z_hi, y), dp: 2 (over z_lo).
Axes of the slice: x: 4, y: 4, z: 4 (z_hi: 2, z_lo: 2; z = z_hi * 2 + z_lo), core: 2. Of those that a mesh axis runs over, the one named last changes fastest.
Arguments:
- activations: bfloat16 [16384, 4096], P(('ctx', 'tp', 'dp')), may hold values from -6 to 6
- out_grad: bfloat16 [16384, 4096], P(('ctx', 'tp', 'dp')), may hold values from -6 to 6
- routes: int32 [16384, 8], P(('ctx', 'tp', 'dp')), may hold values from 0 to 127, all different within a row; in each aligned block of 128 rows (0 to 127, 128 to 255, ...) at most 12 rows name the same one
- gate_probs: bfloat16 [16384, 8], P(('ctx', 'tp', 'dp')), may hold values from 0.049804688 to 0.59765625
- saved_pre: bfloat16 [64, 2, 768, 1536], P(('ctx', 'tp'), 'dp'), may hold values from -6 to 6
- expert_weights: bfloat16 [64, 4096, 2304], P(('ctx', 'tp'), 'dp'), may hold values from -0.09375 to 0.09375
Outputs:
- input_grad: bfloat16 [16384, 4096], P(('ctx', 'tp', 'dp'))
- prob_grad: bfloat16 [16384, 8], P(('ctx', 'tp', 'dp'))
- weight_grad: bfloat16 [64, 4096, 2304], P(('ctx', 'tp'), 'dp')
Inputs may be any that keep to these rules, and one draw needn't show every extreme that they name: `routes`: each row names 8 different experts. Within the rows of one device (aligned blocks of 128 rows) no expert is named more than 12 times, a bound that some block reaches.
All inputs are finite; a program needn't handle non-finite values.
Results may differ from a plain program's by a relative error of at most 0.02.
Values may be sent and summed in bfloat16 or wider, within the bound.
No kernel may reach another device: no remote copies, remote signals or barrier semaphores. Data moves between devices by JAX's collectives and lax.ppermute only.
A program may use at most 192 MiB of HBM per device.

v0:
```python
import jax
import jax.numpy as jnp
from jax import lax
from jax.sharding import PartitionSpec as P


def body(activations, out_grad, routes, gate_probs, saved_pre, expert_weights):
    tok_count = activations.shape[0]
    top_k = routes.shape[1]
    model_width = activations.shape[1]
    ctx_size = lax.axis_size("ctx")
    tp_size = lax.axis_size("tp")
    sources = ctx_size * tp_size
    slots_all = saved_pre.shape[2]
    capacity = slots_all // sources
    hidden = saved_pre.shape[3] // 2
    flat_routes = routes.reshape(-1)
    in_window = flat_routes < sources
    onehot = (flat_routes[:, None] == jnp.arange(sources, dtype=jnp.int32)[None, :]).astype(
        jnp.int32
    )
    position = jnp.sum(jnp.cumsum(onehot, axis=0) * onehot, axis=1) - 1
    slot_index = jnp.where(in_window, flat_routes * capacity + position, sources * capacity)
    route_count = tok_count * top_k
    route_of_slot = jnp.full((sources * capacity,), route_count, jnp.int32)
    route_of_slot = route_of_slot.at[slot_index].set(
        jnp.arange(route_count, dtype=jnp.int32), mode="drop"
    )
    filled = route_of_slot < route_count
    safe_route = jnp.minimum(route_of_slot, route_count - 1)
    token_of_slot = safe_route // top_k
    zero_value = jnp.zeros((), jnp.bfloat16)
    send_rows = jnp.where(filled[:, None], activations[token_of_slot], zero_value)
    send_grads = jnp.where(filled[:, None], out_grad[token_of_slot], zero_value)
    send_probs = jnp.where(filled, gate_probs.reshape(-1)[safe_route], zero_value)
    received = (
        lax.all_to_all(
            send_rows.reshape(sources, capacity, model_width),
            ("ctx", "tp"),
            split_axis=0,
            concat_axis=0,
            tiled=True,
        ),
        lax.all_to_all(
            send_grads.reshape(sources, capacity, model_width),
            ("ctx", "tp"),
            split_axis=0,
            concat_axis=0,
            tiled=True,
        ),
        lax.all_to_all(
            send_probs.reshape(sources, capacity),
            ("ctx", "tp"),
            split_axis=0,
            concat_axis=0,
            tiled=True,
        ),
    )
    recv_rows = received[0].reshape(slots_all, model_width)
    recv_grads = received[1].reshape(slots_all, model_width)
    prob_column = received[2].reshape(slots_all, 1).astype(jnp.float32)
    saved_rows = saved_pre[0, 0]
    pre_gate = saved_rows[:, :hidden].astype(jnp.float32)
    pre_up = saved_rows[:, hidden:].astype(jnp.float32)
    sigmoid_gate = jax.nn.sigmoid(pre_gate)
    activated = pre_gate * sigmoid_gate
    hidden_act = activated * pre_up
    weights = expert_weights[0]
    down_part = weights[:, 2 * hidden :]
    gate_up_part = weights[:, : 2 * hidden]
    down_grad = jnp.dot(
        recv_grads,
        lax.all_gather(down_part, "dp", axis=0, tiled=True),
        preferred_element_type=jnp.float32,
    )
    prob_slot = jnp.sum(hidden_act * down_grad, axis=1).astype(jnp.bfloat16)
    scaled_grad = prob_column * down_grad
    finish_gate_up_grad = jnp.concatenate(
        [
            scaled_grad * pre_up * sigmoid_gate * (1.0 + pre_gate * (1.0 - sigmoid_gate)),
            scaled_grad * activated,
        ],
        axis=1,
    ).astype(jnp.bfloat16)
    finish_scaled_hidden = (prob_column * hidden_act).astype(jnp.bfloat16)
    prob_slot, gate_up_grad, scaled_hidden = (prob_slot, finish_gate_up_grad, finish_scaled_hidden)
    row_grad = lax.dot_general(
        gate_up_grad,
        lax.all_gather(gate_up_part, "dp", axis=0, tiled=True),
        (((1,), (1,)), ((), ())),
        preferred_element_type=jnp.float32,
    ).astype(jnp.bfloat16)
    gate_up_term = lax.dot_general(
        recv_rows, gate_up_grad, (((0,), (0,)), ((), ())), preferred_element_type=jnp.float32
    )
    down_piece = lax.dot_general(
        recv_grads, scaled_hidden, (((0,), (0,)), ((), ())), preferred_element_type=jnp.float32
    )
    weight_grad = lax.psum_scatter(
        jnp.concatenate([gate_up_term, down_piece], axis=1).astype(jnp.bfloat16),
        "dp",
        scatter_dimension=0,
        tiled=True,
    )[None]
    returned = (
        lax.all_to_all(
            row_grad.reshape(sources, capacity, model_width),
            ("ctx", "tp"),
            split_axis=0,
            concat_axis=0,
            tiled=True,
        ),
        lax.all_to_all(
            prob_slot.reshape(sources, capacity),
            ("ctx", "tp"),
            split_axis=0,
            concat_axis=0,
            tiled=True,
        ),
    )
    back_rows = returned[0].reshape(sources * capacity, model_width)
    back_probs = returned[1].reshape(sources * capacity)
    safe_slot = jnp.minimum(slot_index, sources * capacity - 1)
    picked = jnp.where(in_window[:, None], back_rows[safe_slot], zero_value)
    input_grad = jnp.sum(picked.reshape(tok_count, top_k, model_width).astype(jnp.float32), axis=1)
    prob_grad = jnp.where(in_window, back_probs[safe_slot], zero_value).reshape(tok_count, top_k)
    return (input_grad.astype(jnp.bfloat16), prob_grad, weight_grad)


def solution(mesh):
    placed = (
        P(("ctx", "tp", "dp"), None),
        P(("ctx", "tp", "dp"), None),
        P(("ctx", "tp", "dp"), None),
        P(("ctx", "tp", "dp"), None),
        P(("ctx", "tp"), "dp", None, None),
        P(("ctx", "tp"), "dp", None),
    )
    return jax.shard_map(
        body,
        mesh=mesh,
        in_specs=placed,
        out_specs=(
            P(("ctx", "tp", "dp"), None),
            P(("ctx", "tp", "dp"), None),
            P(("ctx", "tp"), "dp", None),
        ),
        check_vma=False,
    )
```

profile of v0, /device:TPU:1, one launch (start us, length us, event | category | flops | bytes accessed | tf_op | source)
XLA Modules:
  0.0 841.0 jit_solution(4453830217344375379)
XLA Ops:
  7.2 0.8 broadcast_multiply_fusion
  8.0 0.8 copy.22
  8.8 0.1 eq.29
  8.8 0.1 eq.25
  9.0 0.4 copy-done.5
  9.4 0.8 copy.28
  10.2 0.1 reshape.169
  10.3 0.1 copy.23
  10.4 0.1 mul.63
  10.5 0.1 lt.57
  10.6 18.0 %reduce-window.6 = s32[64,8,128]{2,1,0:T(8,128)S(1)} reduce-window(s32[64,8,128]{2,1,0:T(8,128)S(1)} %fusion.12, s32[]{:T(128)} %constant.18.clone.1), window={size=1x1x128 pad=0_0x0_0x127_0}, to_apply=%region_0.0 | reduce-window | flops 8323072 | bytes 524292 | tf_op jit(solution)/shard_map/reduce-window
  28.6 0.1 slice.34
  28.8 0.1 copy.26
  29.0 0.1 copy.27
  29.1 0.1 broadcast_add_fusion
  29.2 0.1 fusion.11
  29.3 0.6 compare_select_fusion
  29.9 4.3 scatter_custom_fusion
  34.2 5.0 gather_fusion
  39.2 0.7 all_to_all.25
  40.0 12.3 %all-to-all-start = ((bf16[64,1,12]{2,1,0:T(2,128)(2,1)}), bf16[64,1,12]{2,1,0:T(2,128)(2,1)S(1)}, u32[]{:S(2)}, u32[]{:S(2)}) async-start(bf16[64,1,12]{2,1,0:T(2,128)(2,1)} %all_to_all.25), calls=%async_computation | async-start | bytes 65536 | tf_op jit(solution)/shard_map/all_to_all | solution.py:51
  52.3 0.1 broadcast_in_dim.63
  52.4 5.7 gather_fusion.4
  58.1 9.9 %gather.31 = bf16[64,12,4096]{2,1,0:T(8,128)(2,1)} reshape(bf16[768,4096]{1,0:T(8,128)(2,1)} %gather_fusion.4) | data formatting | bytes 12582912 | tf_op jit(solution)/shard_map/gather | solution.py:33
  68.0 5.7 gather_fusion.1
  73.7 9.7 %gather.25 = bf16[64,12,4096]{2,1,0:T(8,128)(2,1)} reshape(bf16[768,4096]{1,0:T(8,128)(2,1)} %gather_fusion.1) | data formatting | bytes 12582912 | tf_op jit(solution)/shard_map/gather | solution.py:34
  83.5 11.6 %broadcast_select_fusion = (bf16[64,12,4096]{2,1,0:T(8,128)(2,1)}, bf16[64,12,4096]{2,1,0:T(8,128)(2,1)}) fusion(bf16[64,12,4096]{2,1,0:T(8,128)(2,1)} %gather.31, pred[64,12]{1,0:T(8,128)(4,1)S(1)} %broadcast_in_dim.63, bf16[64,12,4096]{2,1,0:T(8,128)(2,1)} %gather.25), kind=kLoop, calls=%fused_computation.10 | loop fusion | flops 6291456 | bytes 25166592 | tf_op jit(solution)/shard_map/jit(_where)/select_n | solution.py:33
  95.0 10.5 %all-to-all-start.4 = ((bf16[64,12,4096]{2,1,0:T(8,128)(2,1)}), bf16[64,12,4096]{2,1,0:T(8,128)(2,1)}, u32[]{:S(2)}, u32[]{:S(2)}) async-start(bf16[64,12,4096]{2,1,0:T(8,128)(2,1)} %get-tuple-element.19), calls=%async_computation.4 | async-start | bytes 16777216 | tf_op jit(solution)/shard_map/all_to_all | solution.py:37
  105.5 0.0 all-gather.3.cloned.1.call-start
  105.6 3.7 slice.36
  109.3 95.8 %all-to-all-done.4 = bf16[64,12,4096]{2,1,0:T(8,128)(2,1)} async-done(((bf16[64,12,4096]{2,1,0:T(8,128)(2,1)}), bf16[64,12,4096]{2,1,0:T(8,128)(2,1)}, u32[]{:S(2)}, u32[]{:S(2)}) %all-to-all-start.4) | async-done | bytes 6291488 | tf_op jit(solution)/shard_map/all_to_all | solution.py:37
  205.1 19.6 %all-to-all-start.1 = ((bf16[64,12,4096]{2,1,0:T(8,128)(2,1)}), bf16[64,12,4096]{2,1,0:T(8,128)(2,1)}, u32[]{:S(2)}, u32[]{:S(2)}) async-start(bf16[64,12,4096]{2,1,0:T(8,128)(2,1)} %get-tuple-element.20), calls=%async_computation.1 | async-start | bytes 16777216 | tf_op jit(solution)/shard_map/all_to_all | solution.py:44
  224.7 0.0 all-gather.5.cloned.1.call-start
  224.7 5.9 slice.39
  230.7 0.5 reduce-scatter.2.cloned.1.call-start
  231.2 1.1 copy-done.3
  232.3 2.5 copy.30
  234.8 0.1 convert_reduce_fusion
  234.9 0.1 reshape.175
  235.0 10.0 %reshape.174 = bf16[768,4096]{1,0:T(8,128)(2,1)} reshape(bf16[64,12,4096]{2,1,0:T(8,128)(2,1)} %all-to-all-done.4) | data formatting | bytes 12582912 | tf_op jit(solution)/shard_map/reshape | solution.py:59
  245.0 79.3 %all-to-all-done.1 = bf16[64,12,4096]{2,1,0:T(8,128)(2,1)} async-done(((bf16[64,12,4096]{2,1,0:T(8,128)(2,1)}), bf16[64,12,4096]{2,1,0:T(8,128)(2,1)}, u32[]{:S(2)}, u32[]{:S(2)}) %all-to-all-start.1) | async-done | bytes 6291488 | tf_op jit(solution)/shard_map/all_to_all | solution.py:44
  324.3 9.8 %reshape.170 = bf16[768,4096]{1,0:T(8,128)(2,1)} reshape(bf16[64,12,4096]{2,1,0:T(8,128)(2,1)} %all-to-all-done.1) | data formatting | bytes 12582912 | tf_op jit(solution)/shard_map/reshape | solution.py:60
  334.1 10.0 %convolution_convert_fusion.1 = bf16[4096,768]{0,1:T(8,128)(2,1)} fusion(bf16[768,4096]{1,0:T(8,128)(2,1)} %reshape.170, f32[768]{0:T(1024)S(1)} %reshape.175, bf16[768,1536]{0,1:T(8,128)(2,1)S(1)} %bitcast.33), kind=kOutput, calls=%fused_computation.12 | convolution fusion | flops 4840292352 | bytes 14945280 | tf_op jit(solution)/shard_map/dot_general | solution.py:96
  344.1 10.4 %all-gather.3.cloned.1.call-done = bf16[4096,768]{1,0:T(8,128)(2,1)} async-done(((bf16[2048,768]{1,0:T(8,128)(2,1)}), bf16[4096,768]{1,0:T(8,128)(2,1)}) %all-gather.3.cloned.1.call-update) | async-done | bytes 6291472 | tf_op jit(solution)/shard_map/all_gather | solution.py:73
  354.5 11.0 %fusion.3 = (bf16[768,768]{0,1:T(8,128)(2,1)S(1)}, bf16[768,768]{0,1:T(8,128)(2,1)}, bf16[768]{0:T(1024)(128)(2,1)S(1)}) fusion(f32[768]{0:T(1024)S(1)} %reshape.175, bf16[768,1536]{0,1:T(8,128)(2,1)S(1)} %bitcast.34, bf16[768,4096]{1,0:T(8,128)(2,1)} %reshape.170, bf16[4096,768]{1,0:T(8,128)(2,1)} %all-gather.3.cloned.1.call-done), kind=kOutput, calls=%fused_computation.21 | convolution fusion | flops 4843043840 | bytes 17306112 | tf_op jit(solution)/shard_map/dot_general | solution.py:71
  365.5 13.5 %convolution_convert_fusion = bf16[4096,1536]{0,1:T(8,128)(2,1)S(1)} fusion(bf16[768,4096]{1,0:T(8,128)(2,1)} %reshape.174, bf16[768,768]{0,1:T(8,128)(2,1)} %get-tuple-element.15, bf16[768,768]{0,1:T(8,128)(2,1)S(1)} %get-tuple-element.14), kind=kOutput, calls=%fused_computation.7 | convolution fusion | flops 9674686464 | bytes 21233664 | tf_op jit(solution)/shard_map/dot_general | solution.py:93
  379.0 17.0 %pad_maximum_fusion = bf16[4096,2304]{0,1:T(8,128)(2,1)} fusion(bf16[4096,768]{0,1:T(8,128)(2,1)} %convolution_convert_fusion.1, bf16[4096,1536]{0,1:T(8,128)(2,1)S(1)} %convolution_convert_fusion), kind=kLoop, calls=%fused_computation.6 | loop fusion | flops 37748736 | bytes 37748736 | tf_op jit(solution)/shard_map/concatenate | solution.py:100
  396.0 0.7 convert_element_type.56
  396.7 11.3 %all-to-all-start.3 = ((bf16[64,1,12]{2,1,0:T(2,128)(2,1)}), bf16[64,1,12]{2,1,0:T(2,128)(2,1)S(1)}, u32[]{:S(2)}, u32[]{:S(2)}) async-start(bf16[64,1,12]{2,1,0:T(2,128)(2,1)} %convert_element_type.56), calls=%async_computation.3 | async-start | bytes 65536 | tf_op jit(solution)/shard_map/all_to_all | solution.py:113
  408.0 105.9 %all-gather.5.cloned.1.call-done = bf16[4096,1536]{1,0:T(8,128)(2,1)} async-done(((bf16[2048,1536]{1,0:T(8,128)(2,1)}), bf16[4096,1536]{1,0:T(8,128)(2,1)}) %all-gather.5.cloned.1.call-update) | async-done | bytes 12582928 | tf_op jit(solution)/shard_map/all_gather | solution.py:89
  513.9 14.7 %convolution_convert_fusion.2 = bf16[768,4096]{1,0:T(8,128)(2,1)} fusion(bf16[4096,1536]{1,0:T(8,128)(2,1)} %all-gather.5.cloned.1.call-done, bf16[768,768]{0,1:T(8,128)(2,1)S(1)} %copy-done.12, bf16[768,768]{0,1:T(8,128)(2,1)S(1)} %copy-done.11), kind=kOutput, calls=%fused_computation.13 | convolution fusion | flops 9671540736 | bytes 21233664 | tf_op jit(solution)/shard_map/dot_general | solution.py:87
  528.6 9.8 %reshape.171 = bf16[64,12,4096]{2,1,0:T(8,128)(2,1)} reshape(bf16[768,4096]{1,0:T(8,128)(2,1)} %convolution_convert_fusion.2) | data formatting | bytes 12582912 | tf_op jit(solution)/shard_map/reshape | solution.py:107
  538.5 11.1 %all-to-all-start.2 = ((bf16[64,12,4096]{2,1,0:T(8,128)(2,1)}), bf16[64,12,4096]{2,1,0:T(8,128)(2,1)}, u32[]{:S(2)}, u32[]{:S(2)}) async-start(bf16[64,12,4096]{2,1,0:T(8,128)(2,1)} %reshape.171), calls=%async_computation.2 | async-start | bytes 16777216 | tf_op jit(solution)/shard_map/all_to_all | solution.py:106
  549.6 0.1 reduce.2
  549.7 0.1 reshape.173
  549.8 6.8 gather_fusion.3
  556.6 0.1 gather.29
  556.7 0.7 copy.32
  557.4 92.3 %all-to-all-done.2 = bf16[64,12,4096]{2,1,0:T(8,128)(2,1)} async-done(((bf16[64,12,4096]{2,1,0:T(8,128)(2,1)}), bf16[64,12,4096]{2,1,0:T(8,128)(2,1)}, u32[]{:S(2)}, u32[]{:S(2)}) %all-to-all-start.2) | async-done | bytes 6291488 | tf_op jit(solution)/shard_map/all_to_all | solution.py:106
  649.7 10.0 %reshape.172 = bf16[768,4096]{1,0:T(8,128)(2,1)} reshape(bf16[64,12,4096]{2,1,0:T(8,128)(2,1)} %all-to-all-done.2) | data formatting | bytes 12582912 | tf_op jit(solution)/shard_map/reshape | solution.py:121
  659.7 18.7 %gather_fusion.2 = bf16[1024,4096]{1,0:T(8,128)(2,1)} fusion(bf16[768,4096]{1,0:T(8,128)(2,1)} %reshape.172, s32[1024]{0:T(1024)S(1)} %broadcast_clamp_fusion), kind=kCustom, calls=%fused_computation.2 | custom fusion | bytes 16781312 | tf_op jit(solution)/shard_map/gather | solution.py:124
  678.3 8.5 %fusion = bf16[128,4096]{1,0:T(8,128)(2,1)} fusion(bf16[1024,4096]{1,0:T(8,128)(2,1)} %gather_fusion.2, pred[128,8]{1,0:T(8,128)(4,1)S(1)} %copy-done.8), kind=kLoop, calls=%fused_computation.9 | loop fusion | flops 7864320 | bytes 9438208 | tf_op jit(solution)/shard_map/reduce_sum | solution.py:125
  686.8 134.7 %reduce-scatter.2.cloned.1.call-done = bf16[2048,2304]{0,1:T(8,128)(2,1)} async-done(((bf16[4096,2304]{0,1:T(8,128)(2,1)}), bf16[2048,2304]{0,1:T(8,128)(2,1)}) %reduce-scatter.2.cloned.1.call-update) | async-done | bytes 9437200 | tf_op jit(solution)/shard_map/reduce_scatter | solution.py:99
  821.5 12.7 %copy.33 = bf16[1,2048,2304]{2,1,0:T(8,128)(2,1)} copy(bf16[1,2048,2304]{1,2,0:T(8,128)(2,1)} %bitcast.32) | data formatting | bytes 18874368
  (40 shorter events, 0.2 us)
Async XLA Ops:
  7.2 45.2 %copy-start = (bf16[128,4096]{1,0:T(8,128)(2,1)S(1)}, bf16[128,4096]{1,0:T(8,128)(2,1)}, u32[]{:S(2)}) copy-start(bf16[128,4096]{1,0:T(8,128)(2,1)} %param.6) | copy-start | bytes 3145732
  8.7 0.6 copy-start.5
  9.4 1.2 copy-start.7
  40.0 55.0 %all-to-all-start = ((bf16[64,1,12]{2,1,0:T(2,128)(2,1)}), bf16[64,1,12]{2,1,0:T(2,128)(2,1)S(1)}, u32[]{:S(2)}, u32[]{:S(2)}) async-start(bf16[64,1,12]{2,1,0:T(2,128)(2,1)} %all_to_all.25), calls=%async_computation | async-start | bytes 65536 | tf_op jit(solution)/shard_map/all_to_all | solution.py:51
  58.1 9.9 %copy-start.2 = (bf16[128,4096]{1,0:T(8,128)(2,1)S(1)}, bf16[128,4096]{1,0:T(8,128)(2,1)}, u32[]{:S(2)}) copy-start(bf16[128,4096]{1,0:T(8,128)(2,1)} %param.7) | copy-start | bytes 3145732
  95.0 110.1 %all-to-all-start.4 = ((bf16[64,12,4096]{2,1,0:T(8,128)(2,1)}), bf16[64,12,4096]{2,1,0:T(8,128)(2,1)}, u32[]{:S(2)}, u32[]{:S(2)}) async-start(bf16[64,12,4096]{2,1,0:T(8,128)(2,1)} %get-tuple-element.19), calls=%async_computation.4 | async-start | bytes 16777216 | tf_op jit(solution)/shard_map/all_to_all | solution.py:37
  105.5 249.0 %all-gather.3.cloned.1.call-start = ((), (), s32[]{:S(2)}) async-start(), calls=%async_computation.6 | async-start | bytes 9437184 | tf_op jit(solution)/shard_map/all_gather | solution.py:73
  205.1 119.2 %all-to-all-start.1 = ((bf16[64,12,4096]{2,1,0:T(8,128)(2,1)}), bf16[64,12,4096]{2,1,0:T(8,128)(2,1)}, u32[]{:S(2)}, u32[]{:S(2)}) async-start(bf16[64,12,4096]{2,1,0:T(8,128)(2,1)} %get-tuple-element.20), calls=%async_computation.1 | async-start | bytes 16777216 | tf_op jit(solution)/shard_map/all_to_all | solution.py:44
  224.7 289.2 %all-gather.5.cloned.1.call-start = ((), (), s32[]{:S(2)}) async-start(), calls=%async_computation.7 | async-start | bytes 18874368 | tf_op jit(solution)/shard_map/all_gather | solution.py:89
  230.6 1.7 copy-start.3
  230.7 590.8 %reduce-scatter.2.cloned.1.call-start = ((), (), s32[]{:S(2)}) async-start(), calls=%async_computation.8 | async-start | bytes 28311552 | tf_op jit(solution)/shard_map/reduce_scatter | solution.py:99
  245.0 89.2 %copy-start.4 = (bf16[1,1,768,1536]{2,3,1,0:T(8,128)(2,1)S(1)}, bf16[1,1,768,1536]{2,3,1,0:T(8,128)(2,1)}, u32[]{:S(2)}) copy-start(bf16[1,1,768,1536]{2,3,1,0:T(8,128)(2,1)} %copy.30) | copy-start | bytes 7077892
  365.5 13.5 %copy-start.10 = (bf16[768,768]{0,1:T(8,128)(2,1)}, bf16[768,768]{0,1:T(8,128)(2,1)S(1)}, u32[]{:S(2)}) copy-start(bf16[768,768]{0,1:T(8,128)(2,1)S(1)} %get-tuple-element.14) | copy-start | bytes 3538948
  395.9 117.9 %copy-start.11 = (bf16[768,768]{0,1:T(8,128)(2,1)S(1)}, bf16[768,768]{0,1:T(8,128)(2,1)}, u32[]{:S(2)}) copy-start(bf16[768,768]{0,1:T(8,128)(2,1)} %copy-done.10) | copy-start | bytes 3538948
  395.9 117.9 %copy-start.12 = (bf16[768,768]{0,1:T(8,128)(2,1)S(1)}, bf16[768,768]{0,1:T(8,128)(2,1)}, u32[]{:S(2)}) copy-start(bf16[768,768]{0,1:T(8,128)(2,1)} %get-tuple-element.15) | copy-start | bytes 3538948
  396.7 141.8 %all-to-all-start.3 = ((bf16[64,1,12]{2,1,0:T(2,128)(2,1)}), bf16[64,1,12]{2,1,0:T(2,128)(2,1)S(1)}, u32[]{:S(2)}, u32[]{:S(2)}) async-start(bf16[64,1,12]{2,1,0:T(2,128)(2,1)} %convert_element_type.56), calls=%async_computation.3 | async-start | bytes 65536 | tf_op jit(solution)/shard_map/all_to_all | solution.py:113
  538.5 11.1 %copy-start.9 = (s32[1024,1]{0,1:T(1,128)S(1)}, s32[1024,1]{0,1:T(1,128)}, u32[]{:S(2)}) copy-start(s32[1024,1]{0,1:T(1,128)} %get-tuple-element.17) | copy-start | bytes 12292
  538.5 18.2 %copy-start.6 = (s32[128,8]{1,0:T(8,128)S(1)}, s32[128,8]{1,0:T(8,128)}, u32[]{:S(2)}) copy-start(s32[128,8]{1,0:T(8,128)} %copy-done.5) | copy-start | bytes 12292
  538.5 111.2 %all-to-all-start.2 = ((bf16[64,12,4096]{2,1,0:T(8,128)(2,1)}), bf16[64,12,4096]{2,1,0:T(8,128)(2,1)}, u32[]{:S(2)}, u32[]{:S(2)}) async-start(bf16[64,12,4096]{2,1,0:T(8,128)(2,1)} %reshape.171), calls=%async_computation.2 | async-start | bytes 16777216 | tf_op jit(solution)/shard_map/all_to_all | solution.py:106
  659.6 18.7 %copy-start.8 = (pred[128,8]{1,0:T(8,128)(4,1)S(1)}, pred[128,8]{1,0:T(8,128)(4,1)}, u32[]{:S(2)}) copy-start(pred[128,8]{1,0:T(8,128)(4,1)} %copy-done.7) | copy-start | bytes 3076
  821.5 12.7 %copy-start.1 = (bf16[128,4096]{1,0:T(8,128)(2,1)S(1)}, bf16[128,4096]{1,0:T(8,128)(2,1)}, u32[]{:S(2)}) copy-start(bf16[128,4096]{1,0:T(8,128)(2,1)} %param.6) | copy-start | bytes 3145732
Sparse Core Ops, SparseCore 0:
  109.4 245.0 all-gather.2
  356.7 157.0 all-gather.4
  516.3 305.1 reduce-scatter.1
where the time goes:
time: 850 us; the launch traced here: 841 us
  waiting for transfers between devices  518 us (61%)
  local copies, waits for them, and re-layouts  137 us (16%)
  starting transfers between devices  65.3 us (8%)
  other arithmetic  56.9 us (7%)
  matrix products  49.2 us (6%)
  between operations  14.2 us (2%)
    reduce_scatter x1, waiting for transfers between devices, body(): lax.psum_scatter(jnp.concatenate([gate_up_term, down_piece], axis=1).asty...  135 us
    all_gather x1, waiting for transfers between devices, body(): lax.all_gather(gate_up_part, 'dp', axis=0, tiled=True)  106 us
    all_to_all x1, waiting for transfers between devices, body(): lax.all_to_all(send_rows.reshape(sources, capacity, model_width), ('ctx',...  95.8 us
    all_to_all x1, waiting for transfers between devices, body(): lax.all_to_all(row_grad.reshape(sources, capacity, model_width), ('ctx',...  92.3 us
    all_to_all x1, waiting for transfers between devices, body(): lax.all_to_all(send_grads.reshape(sources, capacity, model_width), ('ctx'...  79.3 us
    all_to_all x1, starting transfers between devices, body(): lax.all_to_all(send_grads.reshape(sources, capacity, model_width), ('ctx'...  19.6 us
    unnamed x31, local copies, waits for them, and re-layouts  19 us
    gather x1, local copies, waits for them, and re-layouts, body(): picked = jnp.where(in_window[:, None], back_rows[safe_slot], zero_value)  18.7 us
  transfers between devices with their start and end apart: 8, of which 6 were waited for; matrix products, arithmetic and copies ran while one was open for 23% of the time, Pallas kernels for 0%

commit v1 on v0

--- a/solution.py
+++ b/solution.py
@@ -86,7 +86,10 @@
     prob_slot, gate_up_grad, scaled_hidden = (prob_slot, finish_gate_up_grad, finish_scaled_hidden)
     row_grad = lax.dot_general(
         gate_up_grad,
-        lax.all_gather(gate_up_part, "dp", axis=0, tiled=True),
+        jnp.concatenate(
+            lax.all_to_all(jnp.stack([gate_up_part] * lax.axis_size("dp"), axis=0), "dp", 0, 0),
+            axis=0,
+        ),
         (((1,), (1,)), ((), ())),
         preferred_element_type=jnp.float32,
     ).astype(jnp.bfloat16)

time: 850 us -> 923 us (1.086)
  blocking collectives: 0 us -> 107 us
  waiting for transfers between devices: 518 us -> 486 us
  starting transfers between devices: 65.3 us -> 52.1 us
    all_to_all x1, waiting for transfers between devices: 95.8 us -> 272 us  [body(): lax.all_to_all(jnp.stack([gate_up_part] * lax.axis_size('dp'), axis=0), '...]
    reduce_scatter x1, waiting for transfers between devices: 135 us -> 0.01 us  [body(): lax.psum_scatter(jnp.concatenate([gate_up_term, down_piece], axis=1).asty...]
    all_to_all x0 -> x1, blocking collectives: none -> 107 us  [body(): lax.all_to_all(send_rows.reshape(sources, capacity, model_width), ('ctx',...]
    all_gather x1 -> x0, waiting for transfers between devices: 106 us -> none  [body(): lax.all_gather(gate_up_part, 'dp', axis=0, tiled=True)]
    all_gather x1, waiting for transfers between devices: 10.4 us -> 39.6 us  [body(): lax.all_gather(down_part, 'dp', axis=0, tiled=True)]
    all_to_all x1, starting transfers between devices: 19.6 us -> 7.82 us  [body(): lax.all_to_all(send_grads.reshape(sources, capacity, model_width), ('ctx'...]
    another operation x3 -> x4, other arithmetic: 18.2 us -> 23.7 us
  transfers between devices with their start and end apart: 8 -> 7, of which waited for: 6 -> 4; matrix products, arithmetic and copies ran while one was open for 23% -> 17% of each run, Pallas kernels for 0% -> 0%
where the time goes in v1:
time: 923 us; the launch traced here: 905 us
  waiting for transfers between devices  486 us (53%)
  local copies, waits for them, and re-layouts  134 us (15%)
  blocking collectives  107 us (12%)
  other arithmetic  62.5 us (7%)
  starting transfers between devices  52.1 us (6%)
  matrix products  48.4 us (5%)
  between operations  14.6 us (2%)
    all_to_all x1, waiting for transfers between devices, body(): lax.all_to_all(jnp.stack([gate_up_part] * lax.axis_size('dp'), axis=0), '...  272 us
    all_to_all x1, blocking collectives, body(): lax.all_to_all(send_rows.reshape(sources, capacity, model_width), ('ctx',...  107 us
    all_to_all x1, waiting for transfers between devices, body(): lax.all_to_all(row_grad.reshape(sources, capacity, model_width), ('ctx',...  92.5 us
    all_to_all x1, waiting for transfers between devices, body(): lax.all_to_all(send_grads.reshape(sources, capacity, model_width), ('ctx'...  82.3 us
    all_gather x1, waiting for transfers between devices, body(): lax.all_gather(down_part, 'dp', axis=0, tiled=True)  39.6 us
    gather x1, local copies, waits for them, and re-layouts, body(): picked = jnp.where(in_window[:, None], back_rows[safe_slot], zero_value)  18.7 us
  transfers between devices with their start and end apart: 7, of which 4 were waited for; matrix products, arithmetic and copies ran while one was open for 17% of the time, Pallas kernels for 0%

profile of v1, /device:TPU:1, one launch (start us, length us, event | category | flops | bytes accessed | tf_op | source)
XLA Modules:
  0.0 904.9 jit_solution(4698494350534599696)
XLA Ops:
  7.2 0.8 broadcast_multiply_fusion
  8.0 0.8 copy.22
  8.8 0.1 eq.29
  8.8 0.1 eq.25
  9.0 0.4 copy-done.5
  9.4 0.8 copy.28
  10.2 0.1 reshape.172
  10.3 0.1 copy.23
  10.4 0.1 mul.63
  10.5 0.1 lt.57
  10.6 18.0 %reduce-window.6 = s32[64,8,128]{2,1,0:T(8,128)S(1)} reduce-window(s32[64,8,128]{2,1,0:T(8,128)S(1)} %fusion.12, s32[]{:T(128)} %constant.18.clone.1), window={size=1x1x128 pad=0_0x0_0x127_0}, to_apply=%region_0.0 | reduce-window | flops 8323072 | bytes 524292 | tf_op jit(solution)/shard_map/reduce-window
  28.6 0.1 slice.34
  28.8 0.1 copy.26
  29.0 0.1 copy.27
  29.1 0.1 broadcast_add_fusion
  29.2 0.1 fusion.11
  29.3 0.6 compare_select_fusion
  29.9 4.3 scatter_custom_fusion
  34.2 5.0 gather_fusion
  39.2 0.7 all_to_all.29
  40.0 12.3 %all-to-all-start = ((bf16[64,1,12]{2,1,0:T(2,128)(2,1)}), bf16[64,1,12]{2,1,0:T(2,128)(2,1)S(1)}, u32[]{:S(2)}, u32[]{:S(2)}) async-start(bf16[64,1,12]{2,1,0:T(2,128)(2,1)} %all_to_all.29), calls=%async_computation | async-start | bytes 65536 | tf_op jit(solution)/shard_map/all_to_all | solution.py:51
  52.3 0.1 broadcast_in_dim.63
  52.4 5.7 gather_fusion.4
  58.1 9.9 %gather.31 = bf16[64,12,4096]{2,1,0:T(8,128)(2,1)} reshape(bf16[768,4096]{1,0:T(8,128)(2,1)} %gather_fusion.4) | data formatting | bytes 12582912 | tf_op jit(solution)/shard_map/gather | solution.py:33
  68.0 5.7 gather_fusion.1
  73.7 9.8 %gather.25 = bf16[64,12,4096]{2,1,0:T(8,128)(2,1)} reshape(bf16[768,4096]{1,0:T(8,128)(2,1)} %gather_fusion.1) | data formatting | bytes 12582912 | tf_op jit(solution)/shard_map/gather | solution.py:34
  83.5 11.6 %broadcast_select_fusion = (bf16[64,12,4096]{2,1,0:T(8,128)(2,1)}, bf16[64,12,4096]{2,1,0:T(8,128)(2,1)}) fusion(bf16[64,12,4096]{2,1,0:T(8,128)(2,1)} %gather.31, pred[64,12]{1,0:T(8,128)(4,1)S(1)} %broadcast_in_dim.63, bf16[64,12,4096]{2,1,0:T(8,128)(2,1)} %gather.25), kind=kLoop, calls=%fused_computation.11 | loop fusion | flops 6291456 | bytes 25166592 | tf_op jit(solution)/shard_map/jit(_where)/select_n | solution.py:33
  95.1 107.4 %all_to_all.36 = bf16[64,12,4096]{2,1,0:T(8,128)(2,1)} all-to-all(bf16[64,12,4096]{2,1,0:T(8,128)(2,1)} %get-tuple-element.19), channel_id=1, replica_groups=mesh['ctx'=8,'tp'=8,'dp'=2] {'ctx','tp'}, dimensions={0} | all-to-all | bytes 12582912 | tf_op jit(solution)/shard_map/all_to_all | solution.py:37
  202.4 7.8 all-to-all-start.1
  210.3 0.0 all-gather.2.cloned.1.call-start
  210.3 3.9 slice.36
  214.2 0.0 all-gather.2.cloned.1.call-update
  214.2 0.5 reduce-scatter.2.cloned.1.call-start
  214.7 2.5 copy.30
  217.2 0.1 convert_reduce_fusion
  217.3 0.1 reshape.179
  217.4 10.1 %reshape.178 = bf16[768,4096]{1,0:T(8,128)(2,1)} reshape(bf16[64,12,4096]{2,1,0:T(8,128)(2,1)} %all_to_all.36) | data formatting | bytes 12582912 | tf_op jit(solution)/shard_map/reshape | solution.py:59
  227.5 82.3 %all-to-all-done.1 = bf16[64,12,4096]{2,1,0:T(8,128)(2,1)} async-done(((bf16[64,12,4096]{2,1,0:T(8,128)(2,1)}), bf16[64,12,4096]{2,1,0:T(8,128)(2,1)}, u32[]{:S(2)}, u32[]{:S(2)}) %all-to-all-start.1) | async-done | bytes 6291488 | tf_op jit(solution)/shard_map/all_to_all | solution.py:44
  309.8 9.9 %reshape.173 = bf16[768,4096]{1,0:T(8,128)(2,1)} reshape(bf16[64,12,4096]{2,1,0:T(8,128)(2,1)} %all-to-all-done.1) | data formatting | bytes 12582912 | tf_op jit(solution)/shard_map/reshape | solution.py:60
  319.8 9.9 %convolution_convert_fusion.1 = bf16[4096,768]{0,1:T(8,128)(2,1)} fusion(bf16[768,4096]{1,0:T(8,128)(2,1)} %reshape.173, f32[768]{0:T(1024)S(1)} %reshape.179, bf16[768,1536]{0,1:T(8,128)(2,1)S(1)} %bitcast.36), kind=kOutput, calls=%fused_computation.13 | convolution fusion | flops 4840292352 | bytes 14945280 | tf_op jit(solution)/shard_map/dot_general | solution.py:99
  329.7 39.6 %all-gather.2.cloned.1.call-done = bf16[4096,768]{1,0:T(8,128)(2,1)} async-done(((bf16[2048,768]{1,0:T(8,128)(2,1)}), bf16[4096,768]{1,0:T(8,128)(2,1)}) %all-gather.2.cloned.1.call-update) | async-done | bytes 6291472 | tf_op jit(solution)/shard_map/all_gather | solution.py:73
  369.3 11.0 %fusion.3 = (bf16[768,768]{0,1:T(8,128)(2,1)S(1)}, bf16[768,768]{0,1:T(8,128)(2,1)}, bf16[768]{0:T(1024)(128)(2,1)S(1)}) fusion(f32[768]{0:T(1024)S(1)} %reshape.179, bf16[768,1536]{0,1:T(8,128)(2,1)S(1)} %bitcast.37, bf16[768,4096]{1,0:T(8,128)(2,1)} %reshape.173, bf16[4096,768]{1,0:T(8,128)(2,1)} %all-gather.2.cloned.1.call-done), kind=kOutput, calls=%fused_computation.23 | convolution fusion | flops 4843043840 | bytes 17306112 | tf_op jit(solution)/shard_map/dot_general | solution.py:71
  380.3 12.9 %convolution_convert_fusion = bf16[4096,1536]{0,1:T(8,128)(2,1)S(1)} fusion(bf16[768,4096]{1,0:T(8,128)(2,1)} %reshape.178, bf16[768,768]{0,1:T(8,128)(2,1)} %get-tuple-element.15, bf16[768,768]{0,1:T(8,128)(2,1)S(1)} %get-tuple-element.14), kind=kOutput, calls=%fused_computation.7 | convolution fusion | flops 9674686464 | bytes 21233664 | tf_op jit(solution)/shard_map/dot_general | solution.py:96
  393.2 17.0 %pad_maximum_fusion = bf16[4096,2304]{0,1:T(8,128)(2,1)} fusion(bf16[4096,768]{0,1:T(8,128)(2,1)} %convolution_convert_fusion.1, bf16[4096,1536]{0,1:T(8,128)(2,1)S(1)} %convolution_convert_fusion), kind=kLoop, calls=%fused_computation.6 | loop fusion | flops 37748736 | bytes 37748736 | tf_op jit(solution)/shard_map/concatenate | solution.py:103
  410.2 0.0 reduce-scatter.2.cloned.1.call-update
  410.2 3.2 slice_bitcast_fusion
  413.4 5.5 pad_maximum_fusion.1
  418.9 8.8 all-to-all-start.2
  427.7 0.7 convert_element_type.56
  428.5 271.8 %all-to-all-done.2 = bf16[2,2048,1536]{2,1,0:T(8,128)(2,1)} async-done(((bf16[2,2048,1536]{2,1,0:T(8,128)(2,1)}), bf16[2,2048,1536]{2,1,0:T(8,128)(2,1)}, u32[]{:S(2)}, u32[]{:S(2)}) %all-to-all-start.2) | async-done | bytes 12582944 | tf_op jit(solution)/shard_map/all_to_all | solution.py:90
  700.2 11.6 %all-to-all-start.4 = ((bf16[64,1,12]{2,1,0:T(2,128)(2,1)}), bf16[64,1,12]{2,1,0:T(2,128)(2,1)S(1)}, u32[]{:S(2)}, u32[]{:S(2)}) async-start(bf16[64,1,12]{2,1,0:T(2,128)(2,1)} %convert_element_type.56), calls=%async_computation.4 | async-start | bytes 65536 | tf_op jit(solution)/shard_map/all_to_all | solution.py:116
  711.9 14.6 %convolution_convert_fusion.2 = bf16[768,4096]{1,0:T(8,128)(2,1)} fusion(bf16[4096,1536]{1,0:T(8,128)(2,1)} %bitcast.7, bf16[768,768]{0,1:T(8,128)(2,1)S(1)} %copy-done.12, bf16[768,768]{0,1:T(8,128)(2,1)S(1)} %copy-done.11), kind=kOutput, calls=%fused_computation.14 | convolution fusion | flops 9671540736 | bytes 21233664 | tf_op jit(solution)/shard_map/dot_general | solution.py:87
  726.5 10.2 %reshape.175 = bf16[64,12,4096]{2,1,0:T(8,128)(2,1)} reshape(bf16[768,4096]{1,0:T(8,128)(2,1)} %convolution_convert_fusion.2) | data formatting | bytes 12582912 | tf_op jit(solution)/shard_map/reshape | solution.py:110
  736.7 11.1 %all-to-all-start.3 = ((bf16[64,12,4096]{2,1,0:T(8,128)(2,1)}), bf16[64,12,4096]{2,1,0:T(8,128)(2,1)}, u32[]{:S(2)}, u32[]{:S(2)}) async-start(bf16[64,12,4096]{2,1,0:T(8,128)(2,1)} %reshape.175), calls=%async_computation.3 | async-start | bytes 16777216 | tf_op jit(solution)/shard_map/all_to_all | solution.py:109
  747.8 0.1 reduce.2
  747.9 0.1 reshape.177
  748.0 6.8 gather_fusion.3
  754.8 0.1 gather.29
  754.9 0.7 copy.32
  755.6 92.5 %all-to-all-done.3 = bf16[64,12,4096]{2,1,0:T(8,128)(2,1)} async-done(((bf16[64,12,4096]{2,1,0:T(8,128)(2,1)}), bf16[64,12,4096]{2,1,0:T(8,128)(2,1)}, u32[]{:S(2)}, u32[]{:S(2)}) %all-to-all-start.3) | async-done | bytes 6291488 | tf_op jit(solution)/shard_map/all_to_all | solution.py:109
  848.1 9.9 %reshape.176 = bf16[768,4096]{1,0:T(8,128)(2,1)} reshape(bf16[64,12,4096]{2,1,0:T(8,128)(2,1)} %all-to-all-done.3) | data formatting | bytes 12582912 | tf_op jit(solution)/shard_map/reshape | solution.py:124
  858.0 18.7 %gather_fusion.2 = bf16[1024,4096]{1,0:T(8,128)(2,1)} fusion(bf16[768,4096]{1,0:T(8,128)(2,1)} %reshape.176, s32[1024]{0:T(1024)S(1)} %broadcast_clamp_fusion), kind=kCustom, calls=%fused_computation.2 | custom fusion | bytes 16781312 | tf_op jit(solution)/shard_map/gather | solution.py:127
  876.6 8.5 fusion
  885.2 12.7 %copy.33 = bf16[1,2048,2304]{2,1,0:T(8,128)(2,1)} copy(bf16[1,2048,2304]{1,2,0:T(8,128)(2,1)} %bitcast.35) | data formatting | bytes 18874368
  (39 shorter events, 0.2 us)
Async XLA Ops:
  7.2 45.2 %copy-start = (bf16[128,4096]{1,0:T(8,128)(2,1)S(1)}, bf16[128,4096]{1,0:T(8,128)(2,1)}, u32[]{:S(2)}) copy-start(bf16[128,4096]{1,0:T(8,128)(2,1)} %param.6) | copy-start | bytes 3145732
  8.7 0.6 copy-start.5
  9.4 1.2 copy-start.7
  40.0 55.1 %all-to-all-start = ((bf16[64,1,12]{2,1,0:T(2,128)(2,1)}), bf16[64,1,12]{2,1,0:T(2,128)(2,1)S(1)}, u32[]{:S(2)}, u32[]{:S(2)}) async-start(bf16[64,1,12]{2,1,0:T(2,128)(2,1)} %all_to_all.29), calls=%async_computation | async-start | bytes 65536 | tf_op jit(solution)/shard_map/all_to_all | solution.py:51
  58.1 9.9 %copy-start.2 = (bf16[128,4096]{1,0:T(8,128)(2,1)S(1)}, bf16[128,4096]{1,0:T(8,128)(2,1)}, u32[]{:S(2)}) copy-start(bf16[128,4096]{1,0:T(8,128)(2,1)} %param.7) | copy-start | bytes 3145732
  202.4 107.4 %all-to-all-start.1 = ((bf16[64,12,4096]{2,1,0:T(8,128)(2,1)}), bf16[64,12,4096]{2,1,0:T(8,128)(2,1)}, u32[]{:S(2)}, u32[]{:S(2)}) async-start(bf16[64,12,4096]{2,1,0:T(8,128)(2,1)} %get-tuple-element.20), calls=%async_computation.1 | async-start | bytes 16777216 | tf_op jit(solution)/shard_map/all_to_all | solution.py:44
  210.2 4.5 copy-start.3
  210.3 159.1 %all-gather.2.cloned.1.call-start = ((), (), s32[]{:S(2)}) async-start(), calls=%async_computation.7 | async-start | bytes 9437184 | tf_op jit(solution)/shard_map/all_gather | solution.py:73
  214.2 670.9 %reduce-scatter.2.cloned.1.call-start = ((), (), s32[]{:S(2)}) async-start(), calls=%async_computation.8 | async-start | bytes 28311552 | tf_op jit(solution)/shard_map/reduce_scatter | solution.py:102
  227.5 92.3 %copy-start.4 = (bf16[1,1,768,1536]{2,3,1,0:T(8,128)(2,1)S(1)}, bf16[1,1,768,1536]{2,3,1,0:T(8,128)(2,1)}, u32[]{:S(2)}) copy-start(bf16[1,1,768,1536]{2,3,1,0:T(8,128)(2,1)} %copy.30) | copy-start | bytes 7077892
  380.3 12.9 %copy-start.10 = (bf16[768,768]{0,1:T(8,128)(2,1)}, bf16[768,768]{0,1:T(8,128)(2,1)S(1)}, u32[]{:S(2)}) copy-start(bf16[768,768]{0,1:T(8,128)(2,1)S(1)} %get-tuple-element.14) | copy-start | bytes 3538948
  418.9 292.9 %copy-start.11 = (bf16[768,768]{0,1:T(8,128)(2,1)S(1)}, bf16[768,768]{0,1:T(8,128)(2,1)}, u32[]{:S(2)}) copy-start(bf16[768,768]{0,1:T(8,128)(2,1)} %copy-done.10) | copy-start | bytes 3538948
  418.9 293.0 %copy-start.12 = (bf16[768,768]{0,1:T(8,128)(2,1)S(1)}, bf16[768,768]{0,1:T(8,128)(2,1)}, u32[]{:S(2)}) copy-start(bf16[768,768]{0,1:T(8,128)(2,1)} %get-tuple-element.15) | copy-start | bytes 3538948
  418.9 281.3 %all-to-all-start.2 = ((bf16[2,2048,1536]{2,1,0:T(8,128)(2,1)}), bf16[2,2048,1536]{2,1,0:T(8,128)(2,1)}, u32[]{:S(2)}, u32[]{:S(2)}) async-start(bf16[2,2048,1536]{2,1,0:T(8,128)(2,1)} %pad_maximum_fusion.1), calls=%async_computation.2 | async-start | bytes 25165824 | tf_op jit(solution)/shard_map/all_to_all | solution.py:90
  700.2 36.5 %all-to-all-start.4 = ((bf16[64,1,12]{2,1,0:T(2,128)(2,1)}), bf16[64,1,12]{2,1,0:T(2,128)(2,1)S(1)}, u32[]{:S(2)}, u32[]{:S(2)}) async-start(bf16[64,1,12]{2,1,0:T(2,128)(2,1)} %convert_element_type.56), calls=%async_computation.4 | async-start | bytes 65536 | tf_op jit(solution)/shard_map/all_to_all | solution.py:116
  736.7 11.1 %copy-start.9 = (s32[1024,1]{0,1:T(1,128)S(1)}, s32[1024,1]{0,1:T(1,128)}, u32[]{:S(2)}) copy-start(s32[1024,1]{0,1:T(1,128)} %get-tuple-element.17) | copy-start | bytes 12292
  736.7 18.2 %copy-start.6 = (s32[128,8]{1,0:T(8,128)S(1)}, s32[128,8]{1,0:T(8,128)}, u32[]{:S(2)}) copy-start(s32[128,8]{1,0:T(8,128)} %copy-done.5) | copy-start | bytes 12292
  736.7 111.4 %all-to-all-start.3 = ((bf16[64,12,4096]{2,1,0:T(8,128)(2,1)}), bf16[64,12,4096]{2,1,0:T(8,128)(2,1)}, u32[]{:S(2)}, u32[]{:S(2)}) async-start(bf16[64,12,4096]{2,1,0:T(8,128)(2,1)} %reshape.175), calls=%async_computation.3 | async-start | bytes 16777216 | tf_op jit(solution)/shard_map/all_to_all | solution.py:109
  858.0 18.7 %copy-start.8 = (pred[128,8]{1,0:T(8,128)(4,1)S(1)}, pred[128,8]{1,0:T(8,128)(4,1)}, u32[]{:S(2)}) copy-start(pred[128,8]{1,0:T(8,128)(4,1)} %copy-done.7) | copy-start | bytes 3076
  885.2 12.7 %copy-start.1 = (bf16[128,4096]{1,0:T(8,128)(2,1)S(1)}, bf16[128,4096]{1,0:T(8,128)(2,1)}, u32[]{:S(2)}) copy-start(bf16[128,4096]{1,0:T(8,128)(2,1)} %param.6) | copy-start | bytes 3145732
Sparse Core Ops, SparseCore 0:
  214.3 154.9 all-gather.1
  410.3 441.0 reduce-scatter.1
